TPU v7x, 512 devices: a whole 4x4x16 slice. The times are simulated.
512 devices in a mesh: frame: 32 (over x, z_lo), row: 16 (over y, z_hi, core).
Axes of the slice: x: 4, y: 4, z: 16 (z_hi: 2, z_lo: 8; z = z_hi * 8 + z_lo), core: 2. Of those that a mesh axis runs over, the one named last changes fastest.
Arguments:
- tokens: bfloat16 [32, 4096, 512], P('frame', 'row'), may hold values from -15 to 15
- norm_spatial: float32 [512], replicated, may hold values from 0.25 to 1.75
- w_spatial: bfloat16 [512, 1536], replicated, may hold values from -10 to 10
- w_spatial_out: bfloat16 [512, 512], replicated, may hold values from -0.25 to 0.25
- norm_temporal: float32 [512], replicated, may hold values from 0.25 to 1.75
- w_temporal: bfloat16 [512, 1536], replicated, may hold values from -10 to 10
- w_temporal_out: bfloat16 [512, 512], replicated, may hold values from -0.25 to 0.25
Outputs:
- mixed: bfloat16 [32, 4096, 512], P('frame', 'row')
All inputs are finite; a program needn't handle non-finite values.
Results may differ from a plain program's by a relative error of at most 0.01.
The roundings to bfloat16 on the way count: a program that leaves them out, or rounds other values in their place, can miss the bound.
Values may be sent and summed in bfloat16 or wider, within the bound.
No kernel may reach another device: no remote copies, remote signals or barrier semaphores. Data moves between devices by JAX's collectives and lax.ppermute only.
A program may use at most 64 MiB of HBM per device.

v0:
```python
import math

import jax
import jax.numpy as jnp
from jax import lax
from jax.sharding import PartitionSpec as P

HEADS = 8


def layer_norm(rows, gain):
    mean = jnp.mean(rows, axis=-1, keepdims=True)
    centred = rows - mean
    spread = jnp.mean(centred * centred, axis=-1, keepdims=True)
    return centred * lax.rsqrt(spread + 1e-05) * gain


def fold_keys(state, keys, values, query, scale):
    count = keys.shape[0]
    block = math.gcd(count, 512)

    def one_block(index, carry):
        peak, total, summed = carry
        key_rows = lax.dynamic_slice_in_dim(keys, index * block, block, 0)
        value_rows = lax.dynamic_slice_in_dim(values, index * block, block, 0)
        scores = (
            jnp.einsum("qhe,khe->hqk", query, key_rows, preferred_element_type=jnp.float32) * scale
        )
        fresh = jnp.maximum(peak, jnp.max(scores, axis=2))
        fade = jnp.exp(peak - fresh)
        weights = jnp.exp(scores - fresh[:, :, None])
        total = total * fade + jnp.sum(weights, axis=2)
        summed = summed * fade[:, :, None] + jnp.einsum(
            "hqk,khe->hqe",
            weights.astype(jnp.bfloat16),
            value_rows,
            preferred_element_type=jnp.float32,
        )
        return (fresh, total, summed)

    return lax.fori_loop(0, count // block, one_block, state)


def attend_cells(block_qkv):
    frames, cells = (block_qkv.shape[0], block_qkv.shape[1])
    width = block_qkv.shape[2] // 3
    size = width // HEADS
    scale = 1.0 / math.sqrt(size)
    query = block_qkv[:, :, :width].reshape(frames, cells, HEADS, size)
    keys = block_qkv[:, :, width : 2 * width].reshape(frames, cells, HEADS, size)
    values = block_qkv[:, :, 2 * width :].reshape(frames, cells, HEADS, size)
    scores = jnp.einsum("fche,gche->chfg", query, keys, preferred_element_type=jnp.float32) * scale
    later = jnp.arange(frames)[:, None] >= jnp.arange(frames)[None, :]
    scores = jnp.where(later, scores, -1e30)
    peak = jnp.max(scores, axis=3, keepdims=True)
    weights = jnp.exp(scores - peak)
    total = jnp.sum(weights, axis=3)
    summed = jnp.einsum(
        "chfg,gche->fche", weights.astype(jnp.bfloat16), values, preferred_element_type=jnp.float32
    )
    context = summed / jnp.transpose(total, (2, 0, 1))[..., None]
    return context.reshape(frames, cells, width).astype(jnp.bfloat16)


def owner_attend(block_qkv):
    frames, single, cells, triple = block_qkv.shape
    result = attend_cells(block_qkv.reshape(frames, single * cells, triple))
    return result.reshape(frames, single, cells, triple // 3)


def shards(
    tokens, norm_spatial, w_spatial, w_spatial_out, norm_temporal, w_temporal, w_temporal_out
):
    frames_here, rows, width = tokens.shape
    size = width // HEADS
    scale = 1.0 / math.sqrt(size)
    count = frames_here * rows
    resid = tokens.reshape(count, width).astype(jnp.float32)
    normed = layer_norm(resid, norm_spatial).astype(jnp.bfloat16)
    query_flat = jnp.dot(normed, w_spatial[:, :width], preferred_element_type=jnp.float32).astype(
        jnp.bfloat16
    )
    query = query_flat.reshape(count, HEADS, size)
    initial = (
        jnp.full((HEADS, count), -1e30, jnp.float32),
        jnp.zeros((HEADS, count), jnp.float32),
        jnp.zeros((HEADS, count, size), jnp.float32),
    )
    pairs = jnp.dot(normed, w_spatial[:, width:], preferred_element_type=jnp.float32).astype(
        jnp.bfloat16
    )
    piece = lax.all_gather(pairs, "row", axis=0, tiled=True)
    length = piece.shape[0]
    peak, total, summed = fold_keys(
        initial,
        piece[:, :width].reshape(length, HEADS, size),
        piece[:, width:].reshape(length, HEADS, size),
        query,
        scale,
    )
    context = summed / total[:, :, None]
    context = jnp.transpose(context, (1, 0, 2)).reshape(count, width).astype(jnp.bfloat16)
    after = resid + jnp.dot(context, w_spatial_out, preferred_element_type=jnp.float32)
    second = layer_norm(after, norm_temporal).astype(jnp.bfloat16)
    owners = lax.axis_size("frame")
    share = rows // owners
    qkv_t = jnp.dot(second, w_temporal, preferred_element_type=jnp.float32).astype(jnp.bfloat16)
    qkv_t = qkv_t.reshape(frames_here, owners, share, 3 * width)
    gathered = owner_attend(lax.all_to_all(qkv_t, "frame", split_axis=1, concat_axis=0, tiled=True))
    returned = lax.all_to_all(gathered, "frame", split_axis=0, concat_axis=1, tiled=True)
    mixed = after + jnp.dot(
        returned.reshape(count, width), w_temporal_out, preferred_element_type=jnp.float32
    )
    return mixed.reshape(frames_here, rows, width).astype(jnp.bfloat16)


def solution(mesh):
    in_specs = (P("frame", "row", None), P(), P(), P(), P(), P(), P())
    out_specs = P("frame", "row", None)
    return jax.shard_map(shards, mesh=mesh, in_specs=in_specs, out_specs=out_specs, check_vma=False)
```

profile of v0, /device:TPU:1, one launch (start us, length us, event | category | flops | bytes accessed | tf_op | source)
XLA Modules:
  0.0 378.9 jit_solution(7371290148220432065)
XLA Ops:
  6.5 0.0 copy-start
  6.5 0.0 all-gather.2.cloned.1.call-start
  6.5 1.2 convert_reduce_fusion
  7.7 1.2 fusion.29
  8.9 2.7 convolution_convert_fusion.1
  11.6 0.0 all-gather.2.cloned.1.call-update
  11.6 1.5 convolution_convert_fusion.2
  13.1 0.1 copy.24
  13.3 184.6 %all-gather.2.cloned.1.call-done = bf16[4096,1024]{1,0:T(8,128)(2,1)} async-done(((bf16[256,1024]{1,0:T(8,128)(2,1)}), bf16[4096,1024]{1,0:T(8,128)(2,1)}) %all-gather.2.cloned.1.call-update) | async-done | bytes 8388624 | tf_op jit(solution)/shard_map/all_gather | solution.py:92
  197.8 5.7 %fusion.44 = (bf16[4096,512]{1,0:T(8,128)(2,1)}, bf16[4096,512]{1,0:T(8,128)(2,1)}) fusion(bf16[4096,1024]{1,0:T(8,128)(2,1)} %all-gather.2.cloned.1.call-done), kind=kLoop, calls=%fused_computation.62 | loop fusion | bytes 16777216 | tf_op jit(solution)/shard_map/slice | solution.py:97
  203.6 6.4 %copy.23 = bf16[4096,512]{0,1:T(8,128)(2,1)} copy(bf16[4096,512]{1,0:T(8,128)(2,1)} %get-tuple-element.182) | data formatting | bytes 8388608 | tf_op jit(solution)/shard_map/slice | solution.py:96
  210.0 6.5 %copy.25 = bf16[4096,512]{0,1:T(8,128)(2,1)} copy(bf16[4096,512]{1,0:T(8,128)(2,1)} %get-tuple-element.181) | data formatting | bytes 8388608 | tf_op jit(solution)/shard_map/slice | solution.py:97
  216.4 74.1 %while.18 = (s32[]{:T(128)}, f32[8,256]{1,0:T(8,128)S(1)}, f32[8,256]{1,0:T(8,128)S(1)}, f32[8,256,64]{1,2,0:T(8,128)S(1)}, bf16[4096,8,64]{0,2,1:T(8,128)(2,1)}...) while((s32[]{:T(128)}, f32[8,256]{1,0:T(8,128)S(1)}, ...), condition=%wide.region_5.0_spmd.clone, body=%wide.region_2.0_spmd.clone.sunk | while | flops 277227520 | bytes 31850696 | solution.py:41
  216.4 3.9 %bitcast_reduce_fusion.2 = (f32[8,256]{1,0:T(8,128)S(1)}, f32[8,512,256]{2,1,0:T(8,128)}) fusion(bf16[256,8,64]{0,2,1:T(8,128)(2,1)S(1)} %get-tuple-element.268, bf16[4096,8,64]{0,2,1:T(8,128)(2,1)} %get-tuple-element.267, s32[]{:T(128)S(6)} %select_n.16), kind=kOutput, calls=%fused_computation.1.clone.1 | convolution fusion | flops 136312832 | bytes 4988932 | tf_op jit(solution)/shard_map/while/body/eval_jaxpr/qhe,khe->hqk/dot_general | solution.py:27
  220.3 3.0 fusion.62
  223.3 0.4 copy-done.1
  223.7 2.0 fusion.64
  225.8 3.8 bitcast_reduce_fusion.2
  229.5 3.0 fusion.62
  232.6 0.4 copy-done.1
  233.0 2.0 fusion.64
  235.0 3.8 bitcast_reduce_fusion.2
  238.8 3.0 fusion.62
  241.9 0.4 copy-done.1
  242.2 2.0 fusion.64
  244.3 3.8 bitcast_reduce_fusion.2
  248.1 3.0 fusion.62
  251.1 0.4 copy-done.1
  251.5 2.0 fusion.64
  253.5 3.8 bitcast_reduce_fusion.2
  257.3 3.0 fusion.62
  260.4 0.4 copy-done.1
  260.8 2.0 fusion.64
  262.8 3.8 bitcast_reduce_fusion.2
  266.6 3.0 fusion.62
  269.6 0.4 copy-done.1
  270.0 2.0 fusion.64
  272.0 3.8 bitcast_reduce_fusion.2
  275.8 3.0 fusion.62
  278.9 0.4 copy-done.1
  279.3 2.0 fusion.64
  281.3 3.8 bitcast_reduce_fusion.2
  285.1 3.0 fusion.62
  288.1 0.4 copy-done.1
  288.5 2.0 fusion.64
  290.6 0.0 copy-done.2
  290.6 0.0 copy-done.4
  290.6 0.4 fusion.46
  291.0 0.2 multiply_reduce_fusion
  291.3 1.5 fusion.17
  292.8 5.2 %all-to-all-start = ((bf16[1,32,8,1536]{3,2,0,1:T(8,128)(2,1)}), bf16[1,32,8,1536]{3,2,0,1:T(8,128)(2,1)S(1)}, u32[]{:S(2)}, u32[]{:S(2)}) async-start(bf16[1,32,8,1536]{3,2,0,1:T(8,128)(2,1)} %fusion.17), calls=%async_computation | async-start | bytes 1572864 | tf_op jit(solution)/shard_map/all_to_all | solution.py:109
  298.0 39.9 %all-to-all-done = bf16[1,32,8,1536]{3,2,0,1:T(8,128)(2,1)S(1)} async-done(((bf16[1,32,8,1536]{3,2,0,1:T(8,128)(2,1)}), bf16[1,32,8,1536]{3,2,0,1:T(8,128)(2,1)S(1)}, u32[]{:S(2)}, u32[]{:S(2)}) %all-to-all-start) | async-done | bytes 786464 | tf_op jit(solution)/shard_map/all_to_all | solution.py:109
  338.0 0.8 fusion.45
  338.7 1.3 reshape.91
  340.0 1.1 reshape.92
  341.1 1.1 reshape.90
  342.2 1.9 fusion.47
  344.1 0.3 fusion.24
  344.4 1.8 fusion.20
  346.2 0.2 copy.31
  346.4 0.3 convert_element_type.71
  346.7 24.4 %all_to_all.8 = bf16[32,1,8,512]{3,2,1,0:T(8,128)(2,1)S(1)} all-to-all(bf16[32,1,8,512]{3,2,1,0:T(8,128)(2,1)S(1)} %bitcast.73), channel_id=1, replica_groups=mesh['frame'=32,'row'=16] {'frame'}, dimensions={0} | all-to-all | bytes 524288 | tf_op jit(solution)/shard_map/all_to_all | solution.py:110
  371.1 0.0 copy-done.3
  371.1 1.0 fusion.22
  (47 shorter events, 0.3 us)
Async XLA Ops:
  6.5 284.7 %copy-start = (bf16[512,1536]{1,0:T(8,128)(2,1)S(1)}, bf16[512,1536]{1,0:T(8,128)(2,1)}, u32[]{:S(2)}) copy-start(bf16[512,1536]{1,0:T(8,128)(2,1)} %param.14) | copy-start | bytes 4718596
  6.5 191.3 %all-gather.2.cloned.1.call-start = ((), (), s32[]{:S(2)}) async-start(), calls=%async_computation.2 | async-start | bytes 8912896 | tf_op jit(solution)/shard_map/all_gather | solution.py:92
  216.4 74.2 %copy-start.2 = (bf16[1,256,512]{2,1,0:T(8,128)(2,1)S(1)}, bf16[1,256,512]{2,1,0:T(8,128)(2,1)}, u32[]{:S(2)}) copy-start(bf16[1,256,512]{2,1,0:T(8,128)(2,1)} %param.9) | copy-start | bytes 786436
  216.4 74.2 %copy-start.4 = (bf16[512,512]{1,0:T(8,128)(2,1)S(1)}, bf16[512,512]{1,0:T(8,128)(2,1)}, u32[]{:S(2)}) copy-start(bf16[512,512]{1,0:T(8,128)(2,1)} %param.12) | copy-start | bytes 1572868
  216.4 74.8 %copy-start.5 = (f32[512]{0:T(512)S(1)}, f32[512]{0:T(512)}, u32[]{:S(2)}) copy-start(f32[512]{0:T(512)} %param.13) | copy-start | bytes 6148
  220.3 3.4 copy-start.1
  229.5 3.4 copy-start.1
  238.8 3.4 copy-start.1
  248.1 3.4 copy-start.1
  257.3 3.4 copy-start.1
  266.6 3.4 copy-start.1
  275.8 3.4 copy-start.1
  285.1 3.4 copy-start.1
  292.8 45.2 %all-to-all-start = ((bf16[1,32,8,1536]{3,2,0,1:T(8,128)(2,1)}), bf16[1,32,8,1536]{3,2,0,1:T(8,128)(2,1)S(1)}, u32[]{:S(2)}, u32[]{:S(2)}) async-start(bf16[1,32,8,1536]{3,2,0,1:T(8,128)(2,1)} %fusion.17), calls=%async_computation | async-start | bytes 1572864 | tf_op jit(solution)/shard_map/all_to_all | solution.py:109
  344.1 27.0 %copy-start.3 = (bf16[512,512]{1,0:T(8,128)(2,1)S(1)}, bf16[512,512]{1,0:T(8,128)(2,1)}, u32[]{:S(2)}) copy-start(bf16[512,512]{1,0:T(8,128)(2,1)} %param.15) | copy-start | bytes 1572868
Sparse Core Ops, SparseCore 0:
  11.7 186.0 all-gather.1
where the time goes:
time: 380 us; the launch traced here: 379 us
  waiting for transfers between devices  225 us (59%)
  matrix products  57 us (15%)
  other arithmetic  27.3 us (7%)
  local copies, waits for them, and re-layouts  26.6 us (7%)
  blocking collectives  24.4 us (6%)
  between operations  13.6 us (4%)
  starting transfers between devices  5.24 us (1%)
    all_gather x1, waiting for transfers between devices, shards(): piece = lax.all_gather(pairs, 'row', axis=0, tiled=True)  185 us
    all_to_all x1, waiting for transfers between devices, shards(): lax.all_to_all(qkv_t, 'frame', split_axis=1, concat_axis=0, tiled=True)  39.9 us
    dot_general x8, matrix products, one_block(): jnp.einsum('qhe,khe->hqk', query, key_rows, preferred_element_type=jnp.fl...  30.4 us
    all_to_all x1, blocking collectives, shards(): lax.all_to_all(gathered, 'frame', split_axis=0, concat_axis=1, tiled=True)  24.4 us
    reduce_sum x8, other arithmetic, one_block(): total = total * fade + jnp.sum(weights, axis=2)  24.2 us
    dot_general x8, matrix products, one_block(): jnp.einsum('hqk,khe->hqe', weights.astype(jnp.bfloat16), value_rows, pref...  15.8 us
    slice x2, local copies, waits for them, and re-layouts, shards(): piece[:, width:].reshape(length, HEADS, size)  12.2 us
  transfers between devices with their start and end apart: 2, of which 2 were waited for; matrix products, arithmetic and copies ran while one was open for 0% of the time, Pallas kernels for 0%

commit v1 on v0

v1 whole, which is shorter than its diff:
```python
import math

import jax
import jax.numpy as jnp
from jax import lax
from jax.experimental import pallas as pl
from jax.experimental.pallas import tpu as pltpu
from jax.sharding import Mesh
from jax.sharding import PartitionSpec as P

HEADS = 8
PAIR = 2


def layer_norm(rows, gain):
    mean = jnp.mean(rows, axis=-1, keepdims=True)
    centred = rows - mean
    spread = jnp.mean(centred * centred, axis=-1, keepdims=True)
    return centred * lax.rsqrt(spread + 1e-05) * gain


def spatial_kernel(q_ref, k_ref, v_ref, o_ref, *, size, scale):
    for h in range(PAIR):
        cols = slice(h * size, (h + 1) * size)
        query = q_ref[:, cols]
        keys = k_ref[:, cols]
        values = v_ref[:, cols]
        scores = (
            lax.dot_general(
                query, keys, (((1,), (1,)), ((), ())), preferred_element_type=jnp.float32
            )
            * scale
        )
        peak = jnp.max(scores, axis=1, keepdims=True)
        weights = jnp.exp(scores - peak)
        total = jnp.sum(weights, axis=1, keepdims=True)
        summed = jnp.dot(
            weights.astype(jnp.bfloat16), values, preferred_element_type=jnp.float32
        )
        o_ref[:, cols] = (summed / total).astype(o_ref.dtype)


def spatial_attention(query, keys, values):
    count, width = query.shape
    length = keys.shape[0]
    size = width // HEADS
    block = PAIR * size
    kernel = lambda *refs: spatial_kernel(*refs, size=size, scale=1.0 / math.sqrt(size))
    return pl.pallas_call(
        kernel,
        grid=(width // block,),
        in_specs=[
            pl.BlockSpec((count, block), lambda h: (0, h)),
            pl.BlockSpec((length, block), lambda h: (0, h)),
            pl.BlockSpec((length, block), lambda h: (0, h)),
        ],
        out_specs=pl.BlockSpec((count, block), lambda h: (0, h)),
        out_shape=jax.ShapeDtypeStruct((count, width), jnp.bfloat16),
        compiler_params=pltpu.CompilerParams(vmem_limit_bytes=48 * 1024 * 1024),
    )(query, keys, values)


def attend_cells(block_qkv):
    frames, cells = (block_qkv.shape[0], block_qkv.shape[1])
    width = block_qkv.shape[2] // 3
    size = width // HEADS
    scale = 1.0 / math.sqrt(size)
    query = block_qkv[:, :, :width].reshape(frames, cells, HEADS, size)
    keys = block_qkv[:, :, width : 2 * width].reshape(frames, cells, HEADS, size)
    values = block_qkv[:, :, 2 * width :].reshape(frames, cells, HEADS, size)
    scores = jnp.einsum("fche,gche->chfg", query, keys, preferred_element_type=jnp.float32) * scale
    later = jnp.arange(frames)[:, None] >= jnp.arange(frames)[None, :]
    scores = jnp.where(later, scores, -1e30)
    peak = jnp.max(scores, axis=3, keepdims=True)
    weights = jnp.exp(scores - peak)
    total = jnp.sum(weights, axis=3)
    summed = jnp.einsum(
        "chfg,gche->fche", weights.astype(jnp.bfloat16), values, preferred_element_type=jnp.float32
    )
    context = summed / jnp.transpose(total, (2, 0, 1))[..., None]
    return context.reshape(frames, cells, width).astype(jnp.bfloat16)


def shards(
    tokens, norm_spatial, w_spatial, w_spatial_out, norm_temporal, w_temporal, w_temporal_out
):
    frames_here, rows, width = tokens.shape
    count = frames_here * rows
    resid = tokens.reshape(count, width).astype(jnp.float32)
    normed = layer_norm(resid, norm_spatial).astype(jnp.bfloat16)
    query = jnp.dot(normed, w_spatial[:, :width], preferred_element_type=jnp.float32).astype(
        jnp.bfloat16
    )
    piece = lax.all_gather(normed, "core", axis=0, tiled=True)
    piece = lax.all_gather(piece, "zhi", axis=0, tiled=True)
    piece = lax.all_gather(piece, "y", axis=0, tiled=True)
    pairs = jnp.dot(piece, w_spatial[:, width:], preferred_element_type=jnp.float32).astype(
        jnp.bfloat16
    )
    context = spatial_attention(query, pairs[:, :width], pairs[:, width:])
    after = resid + jnp.dot(context, w_spatial_out, preferred_element_type=jnp.float32)
    second = layer_norm(after, norm_temporal).astype(jnp.bfloat16)
    owners = lax.axis_size(("x", "zlo"))
    share = rows // owners
    second = second.reshape(frames_here, owners, share, width)
    gathered = lax.all_to_all(second, ("x", "zlo"), split_axis=1, concat_axis=0, tiled=True)
    frames_all = gathered.shape[0]
    qkv_t = jnp.dot(
        gathered.reshape(frames_all * share, width), w_temporal, preferred_element_type=jnp.float32
    ).astype(jnp.bfloat16)
    context_t = attend_cells(qkv_t.reshape(frames_all, share, 3 * width))
    context_t = context_t.reshape(frames_all, 1, share, width)
    returned = lax.all_to_all(context_t, ("x", "zlo"), split_axis=0, concat_axis=1, tiled=True)
    mixed = after + jnp.dot(
        returned.reshape(count, width), w_temporal_out, preferred_element_type=jnp.float32
    )
    return mixed.reshape(frames_here, rows, width).astype(jnp.bfloat16)


def solution(mesh):
    frame_n, row_n = mesh.devices.shape
    devices = mesh.devices.reshape(4, frame_n // 4, row_n // 4, 2, 2)
    fine = Mesh(devices, ("x", "zlo", "y", "zhi", "core"))
    grid_spec = P(("x", "zlo"), ("y", "zhi", "core"), None)
    in_specs = (grid_spec, P(), P(), P(), P(), P(), P())
    return jax.shard_map(shards, mesh=fine, in_specs=in_specs, out_specs=grid_spec, check_vma=False)
```

time: 380 us -> 239 us (0.63)
  waiting for transfers between devices: 225 us -> 141 us
  matrix products: 57 us -> 13 us
  other arithmetic: 27.3 us -> 4.85 us
  local copies, waits for them, and re-layouts: 26.6 us -> 4.68 us
  Pallas kernels: 0 us -> 16.5 us
  blocking collectives: 24.4 us -> 32.7 us
  starting transfers between devices: 5.24 us -> 12.7 us
    all_gather x1 -> x2, waiting for transfers between devices: 185 us -> 122 us  [the longest x1 70.2 us: shards(): piece = lax.all_gather(piece, 'zhi', axis=0, tiled=True)]
    dot_general x18 -> x2, matrix products: 50.4 us -> 7.58 us  [the longest x1 7.01 us: shards(): jnp.dot(piece, w_spatial[:, width:], preferred_element_type=jnp.float32)]
    reduce_sum x8 -> x0, other arithmetic: 24.2 us -> none  [one_block(): total = total * fade + jnp.sum(weights, axis=2)]
    all_to_all x1, waiting for transfers between devices: 39.9 us -> 18.6 us  [shards(): lax.all_to_all(second, ('x', 'zlo'), split_axis=1, concat_axis=0, tiled=T...]
    pallas_call x0 -> x1, Pallas kernels: none -> 16.5 us  [spatial_attention(): pl.pallas_call(kernel, grid=(width // block,), in_specs=[pl.BlockSpec((co...]
    slice x3 -> x1, local copies, waits for them, and re-layouts: 18.6 us -> 2.46 us  [shards(): context = spatial_attention(query, pairs[:, :width], pairs[:, width:])]
    all_gather x0 -> x1, blocking collectives: none -> 8.78 us  [shards(): piece = lax.all_gather(normed, 'core', axis=0, tiled=True)]
    all_to_all x1, starting transfers between devices: 5.23 us -> 12.7 us  [shards(): lax.all_to_all(second, ('x', 'zlo'), split_axis=1, concat_axis=0, tiled=T...]
  transfers between devices with their start and end apart: 2 -> 3, of which waited for: 2 -> 3; matrix products, arithmetic and copies ran while one was open for 0% -> 1% of each run, Pallas kernels for 0% -> 0%
where the time goes in v1:
time: 239 us
  waiting for transfers between devices  141 us (59%)
  blocking collectives  32.7 us (14%)
  Pallas kernels  16.5 us (7%)
  between operations  13.6 us (6%)
  matrix products  13 us (5%)
  starting transfers between devices  12.7 us (5%)
  other arithmetic  4.85 us (2%)
  local copies, waits for them, and re-layouts  4.68 us (2%)
    all_gather x1, waiting for transfers between devices, shards(): piece = lax.all_gather(piece, 'zhi', axis=0, tiled=True)  70.2 us
    all_gather x1, waiting for transfers between devices, shards(): piece = lax.all_gather(piece, 'y', axis=0, tiled=True)  51.9 us
    all_to_all x1, blocking collectives, shards(): lax.all_to_all(context_t, ('x', 'zlo'), split_axis=0, concat_axis=1, tile...  23.9 us
    all_to_all x1, waiting for transfers between devices, shards(): lax.all_to_all(second, ('x', 'zlo'), split_axis=1, concat_axis=0, tiled=T...  18.6 us
    pallas_call x1, Pallas kernels, spatial_attention(): pl.pallas_call(kernel, grid=(width // block,), in_specs=[pl.BlockSpec((co...  16.5 us
    all_to_all x1, starting transfers between devices, shards(): lax.all_to_all(second, ('x', 'zlo'), split_axis=1, concat_axis=0, tiled=T...  12.7 us
    all_gather x1, blocking collectives, shards(): piece = lax.all_gather(normed, 'core', axis=0, tiled=True)  8.78 us
    dot_general x1, matrix products, shards(): jnp.dot(piece, w_spatial[:, width:], preferred_element_type=jnp.float32)  7.01 us
  transfers between devices with their start and end apart: 3, of which 3 were waited for; matrix products, arithmetic and copies ran while one was open for 1% of the time, Pallas kernels for 0%

profile of v1, /device:TPU:1, one launch (start us, length us, event | category | flops | bytes accessed | tf_op | source)
XLA Modules:
  0.0 238.7 jit_solution(5829038435156929912)
XLA Ops:
  6.5 0.0 copy-start
  6.5 0.0 all-gather.3.cloned.1.call-start
  6.5 1.2 convert_reduce_fusion
  7.7 1.2 fusion.12
  8.9 1.1 fusion.14
  10.0 8.8 %all_gather.9 = bf16[512,512]{1,0:T(8,128)(2,1)} all-gather(bf16[256,512]{1,0:T(8,128)(2,1)S(1)} %fusion.14), channel_id=1, replica_groups=mesh['x'=4,'zlo'=8,'y'=4,'zhi'=2,'core'=2] {'core'}, dimensions={0}, use_global_device_ids=true | all-gather | bytes 786432 | tf_op jit(solution)/shard_map/all_gather | solution.py:94
  18.8 0.0 all-gather.3.cloned.1.call-update
  18.8 0.0 all-gather.5.cloned.1.call-start
  18.9 70.2 %all-gather.3.cloned.1.call-done = bf16[1024,512]{1,0:T(8,128)(2,1)} async-done(((bf16[512,512]{1,0:T(8,128)(2,1)}), bf16[1024,512]{1,0:T(8,128)(2,1)}) %all-gather.3.cloned.1.call-update) | async-done | bytes 1048592 | tf_op jit(solution)/shard_map/all_gather | solution.py:95
  89.1 0.0 all-gather.5.cloned.1.call-update
  89.1 1.3 convolution_convert_fusion.2.refs_0_
  90.5 51.9 %all-gather.5.cloned.1.call-done = bf16[4096,512]{1,0:T(8,128)(2,1)} async-done(((bf16[1024,512]{1,0:T(8,128)(2,1)}), bf16[4096,512]{1,0:T(8,128)(2,1)}) %all-gather.5.cloned.1.call-update) | async-done | bytes 4194320 | tf_op jit(solution)/shard_map/all_gather | solution.py:96
  142.4 7.0 %convolution_convert_fusion = bf16[4096,1024]{1,0:T(8,128)(2,1)S(1)} fusion(bf16[4096,512]{1,0:T(8,128)(2,1)} %all-gather.5.cloned.1.call-done, bf16[512,1536]{1,0:T(8,128)(2,1)} %param.9), kind=kOutput, calls=%fused_computation | convolution fusion | flops 4299161600 | bytes 13631488 | tf_op jit(solution)/shard_map/dot_general | solution.py:97
  149.4 2.5 %fusion.24 = (bf16[4096,512]{1,0:T(8,128)(2,1)}, bf16[4096,512]{1,0:T(8,128)(2,1)S(1)}) fusion(bf16[4096,1024]{1,0:T(8,128)(2,1)S(1)} %convolution_convert_fusion), kind=kLoop, calls=%fused_computation.40 | loop fusion | bytes 16777216 | tf_op jit(solution)/shard_map/slice | solution.py:100
  151.9 0.0 copy-start.1
  151.9 0.0 copy-start.3
  151.9 0.0 copy-start.4
  151.9 16.5 %shard_map.73 = bf16[256,512]{1,0:T(8,128)(2,1)S(1)} custom-call(bf16[256,512]{1,0:T(8,128)(2,1)S(1)} %convolution_convert_fusion.2.refs_0_, bf16[4096,512]{1,0:T(8,128)(2,1)S(1)} %get-tuple-element.6.refs_1_, bf16[4096,512]{1,0:T(8,128)(2,1)} %get-tuple-element.5.refs_2_), custom_call_target="tpu_custom_call" | custom-call | tf_op jit(solution)/shard_map/pallas_call | solution.py:49
  168.4 0.0 copy-done.1
  168.4 0.0 copy-done.3
  168.4 0.4 fusion.26
  168.8 0.2 multiply_reduce_fusion
  169.0 0.0 copy-done.4
  169.0 0.9 fusion.21
  169.9 12.7 %all-to-all-start = ((bf16[1,32,8,512]{3,2,0,1:T(8,128)(2,1)}), bf16[1,32,8,512]{3,2,0,1:T(8,128)(2,1)S(1)}, u32[]{:S(2)}, u32[]{:S(2)}) async-start(bf16[1,32,8,512]{3,2,0,1:T(8,128)(2,1)} %fusion.21), calls=%async_computation | async-start | bytes 524288 | tf_op jit(solution)/shard_map/all_to_all | solution.py:106
  182.6 18.6 %all-to-all-done = bf16[1,32,8,512]{3,2,0,1:T(8,128)(2,1)S(1)} async-done(((bf16[1,32,8,512]{3,2,0,1:T(8,128)(2,1)}), bf16[1,32,8,512]{3,2,0,1:T(8,128)(2,1)S(1)}, u32[]{:S(2)}, u32[]{:S(2)}) %all-to-all-start) | async-done | bytes 262176 | tf_op jit(solution)/shard_map/all_to_all | solution.py:106
  201.2 0.0 copy-done
  201.2 0.6 fusion
  201.8 0.1 fusion.25
  201.8 0.3 reshape.78
  202.1 1.1 reshape.79
  203.2 0.3 reshape.77
  203.5 1.9 fusion.27
  205.4 0.0 copy-start.2
  205.4 0.3 fusion.7
  205.7 0.8 fusion.3
  206.4 0.2 copy.19
  206.7 0.3 convert_element_type.52
  207.0 23.9 %all_to_all.8 = bf16[32,1,8,512]{3,2,1,0:T(8,128)(2,1)S(1)} all-to-all(bf16[32,1,8,512]{3,2,1,0:T(8,128)(2,1)S(1)} %bitcast.46), channel_id=1, replica_groups=mesh['x'=4,'zlo'=8,'y'=4,'zhi'=2,'core'=2] {'x','zlo'}, dimensions={0} | all-to-all | bytes 524288 | tf_op jit(solution)/shard_map/all_to_all | solution.py:113
  230.9 0.0 copy-done.2
  230.9 1.0 fusion.5
  (5 shorter events, 0.0 us)
Async XLA Ops:
  6.5 194.7 %copy-start = (bf16[512,1536]{1,0:T(8,128)(2,1)S(1)}, bf16[512,1536]{1,0:T(8,128)(2,1)}, u32[]{:S(2)}) copy-start(bf16[512,1536]{1,0:T(8,128)(2,1)} %param.12) | copy-start | bytes 4718596
  6.5 82.6 %all-gather.3.cloned.1.call-start = ((), (), s32[]{:S(2)}) async-start(), calls=%async_computation.2 | async-start | bytes 1572864 | tf_op jit(solution)/shard_map/all_gather | solution.py:95
  18.8 123.5 %all-gather.5.cloned.1.call-start = ((), (), s32[]{:S(2)}) async-start(), calls=%async_computation.3 | async-start | bytes 5242880 | tf_op jit(solution)/shard_map/all_gather | solution.py:96
  151.9 16.5 %copy-start.1 = (bf16[1,256,512]{2,1,0:T(8,128)(2,1)S(1)}, bf16[1,256,512]{2,1,0:T(8,128)(2,1)}, u32[]{:S(2)}) copy-start(bf16[1,256,512]{2,1,0:T(8,128)(2,1)} %param.7) | copy-start | bytes 786436
  151.9 16.5 %copy-start.3 = (bf16[512,512]{1,0:T(8,128)(2,1)S(1)}, bf16[512,512]{1,0:T(8,128)(2,1)}, u32[]{:S(2)}) copy-start(bf16[512,512]{1,0:T(8,128)(2,1)} %param.10) | copy-start | bytes 1572868
  151.9 17.1 %copy-start.4 = (f32[512]{0:T(512)S(1)}, f32[512]{0:T(512)}, u32[]{:S(2)}) copy-start(f32[512]{0:T(512)} %param.11) | copy-start | bytes 6148
  169.9 31.3 %all-to-all-start = ((bf16[1,32,8,512]{3,2,0,1:T(8,128)(2,1)}), bf16[1,32,8,512]{3,2,0,1:T(8,128)(2,1)S(1)}, u32[]{:S(2)}, u32[]{:S(2)}) async-start(bf16[1,32,8,512]{3,2,0,1:T(8,128)(2,1)} %fusion.21), calls=%async_computation | async-start | bytes 524288 | tf_op jit(solution)/shard_map/all_to_all | solution.py:106
  205.4 25.5 %copy-start.2 = (bf16[512,512]{1,0:T(8,128)(2,1)S(1)}, bf16[512,512]{1,0:T(8,128)(2,1)}, u32[]{:S(2)}) copy-start(bf16[512,512]{1,0:T(8,128)(2,1)} %param.13) | copy-start | bytes 1572868
Sparse Core Ops, SparseCore 0:
  19.0 70.0 all-gather.2
  91.2 51.1 all-gather.4
